TPU v7x, 128 devices: a whole 4x4x4 slice. The times are simulated.
128 devices in a mesh: src: 16 (over y_lo, z, core), tgt: 8 (over y_hi, x).
Axes of the slice: x: 4, y: 4 (y_hi: 2, y_lo: 2; y = y_hi * 2 + y_lo), z: 4, core: 2. Of those that a mesh axis runs over, the one named last changes fastest.
Arguments:
- src_emb: bfloat16 [16384, 768], P(('src', 'tgt')), may hold values from -0.05119037 to 0.05119037
- right_sentence_vectors: bfloat16 [8192, 768], P(('tgt', 'src')), may hold values from -0.05119037 to 0.05119037
- src_mass: float32 [16384], P('src'), may hold values from 0.25 to 4
- tgt_mass: float32 [8192], P('tgt'), may hold values from 0.5 to 8
Outputs:
- grad_src: float32 [16384, 768], P(('src', 'tgt'))
- grad_tgt: float32 [8192, 768], P(('tgt', 'src'))
All inputs are finite; a program needn't handle non-finite values.
Results may differ from a plain program's by a relative error of at most 0.00045.
Values may be sent and summed in bfloat16 or wider, within the bound.
No kernel may reach another device: no remote copies, remote signals or barrier semaphores. Data moves between devices by JAX's collectives and lax.ppermute only.
A program may use at most 64 MiB of HBM per device.

v0:
```python
import jax
import jax.numpy as jnp
from jax import lax
from jax.sharding import PartitionSpec as P

ITERS = 4
regularizer_epsilon = 0.05
highest = lax.Precision.HIGHEST


def row_total(part):
    return lax.psum(part, "tgt")


def col_total(part):
    return lax.psum(part, "src")


def times_vector(kernel, vector):
    return jnp.dot(kernel, vector, precision=highest, preferred_element_type=jnp.float32)


def vector_times(vector, kernel):
    return jnp.dot(vector, kernel, precision=highest, preferred_element_type=jnp.float32)


def per_device(src_emb, right_sentence_vectors, src_mass, tgt_mass):
    src_rows = lax.all_gather(src_emb, "tgt", axis=0, tiled=True)
    target_rows = lax.all_gather(right_sentence_vectors, "src", axis=0, tiled=True)

    def build():
        kernel_grid = (
            lax.dot_general(
                src_rows, target_rows, (((1,), (1,)), ((), ())), preferred_element_type=jnp.float32
            )
            / regularizer_epsilon
        )
        kernel = lax.optimization_barrier(jnp.exp(kernel_grid).astype(jnp.bfloat16))
        return (kernel_grid, kernel)

    kernel_grid, kernel = build()
    vector = jnp.ones(tgt_mass.shape, jnp.float32)
    old_saved, row_saved, src_saved, col_saved, tgt_saved = ([], [], [], [], [])
    for iteration in range(ITERS):
        old_saved.append(vector)
        row_sum = row_total(times_vector(kernel, vector))
        src_scale = src_mass / row_sum
        col_sum = col_total(vector_times(src_scale, kernel))
        vector = tgt_mass / col_sum
        row_saved.append(row_sum)
        src_saved.append(src_scale)
        col_saved.append(col_sum)
        tgt_saved.append(vector)
    last_src = src_saved[-1]
    last_tgt = tgt_saved[-1]
    weighted = kernel * kernel_grid
    src_adj = row_total(times_vector(weighted, last_tgt))
    tgt_adj = col_total(vector_times(last_src, weighted))
    row_bars = [None] * ITERS
    col_bars = [None] * ITERS
    for iteration in reversed(range(ITERS)):
        kernel_grid, kernel = build()
        col_bar = -tgt_adj * tgt_saved[iteration] / col_saved[iteration]
        back = row_total(times_vector(kernel, col_bar))
        if iteration == ITERS - 1:
            back = back + src_adj
        row_bar = -back * src_saved[iteration] / row_saved[iteration]
        if iteration > 0:
            tgt_adj = col_total(vector_times(row_bar, kernel))
        row_bars[iteration] = row_bar
        col_bars[iteration] = col_bar
    left = jnp.stack(row_bars + src_saved, axis=1)
    right = jnp.stack(old_saved + col_bars, axis=1)
    lowrank = lax.dot_general(
        left, right, (((1,), (1,)), ((), ())), precision=highest, preferred_element_type=jnp.float32
    )
    cross_term_grid = (
        kernel * (last_src[:, None] * last_tgt[None, :] * (1.0 + kernel_grid) + lowrank)
    ).astype(jnp.bfloat16)
    left_share_piece = (
        jnp.dot(cross_term_grid, target_rows, preferred_element_type=jnp.float32)
        / regularizer_epsilon
    )
    right_share_piece = (
        lax.dot_general(
            cross_term_grid, src_rows, (((0,), (0,)), ((), ())), preferred_element_type=jnp.float32
        )
        / regularizer_epsilon
    )
    src_whole = lax.psum(left_share_piece, "tgt")
    tgt_whole = lax.psum(right_share_piece, "src")
    src_count = src_emb.shape[0]
    tgt_count = right_sentence_vectors.shape[0]
    grad_src = lax.dynamic_slice_in_dim(src_whole, lax.axis_index("tgt") * src_count, src_count, 0)
    grad_tgt = lax.dynamic_slice_in_dim(tgt_whole, lax.axis_index("src") * tgt_count, tgt_count, 0)
    return (grad_src, grad_tgt)


def solution(mesh):
    placed = (P(("src", "tgt"), None), P(("tgt", "src"), None), P("src"), P("tgt"))
    return jax.shard_map(
        per_device,
        mesh=mesh,
        in_specs=placed,
        out_specs=(P(("src", "tgt"), None), P(("tgt", "src"), None)),
        check_vma=False,
    )
```

profile of v0, /device:TPU:1, one launch (start us, length us, event | category | flops | bytes accessed | tf_op | source)
XLA Modules:
  0.0 730.8 jit_solution(13594640266932629747)
XLA Ops:
  7.2 0.7 all-gather.3.cloned.1.call-update
  7.9 0.7 all-gather.5.cloned.1.call-update
  8.7 54.5 %all-gather.3.cloned.1.call-done = bf16[1024,768]{1,0:T(8,128)(2,1)} async-done(((bf16[128,768]{1,0:T(8,128)(2,1)}), bf16[1024,768]{1,0:T(8,128)(2,1)}) %all-gather.3.cloned.1.call-update) | async-done | bytes 1572880 | tf_op jit(solution)/shard_map/all_gather | solution.py:28
  63.2 35.8 %all-gather.5.cloned.1.call-done = bf16[1024,768]{1,0:T(8,128)(2,1)} async-done(((bf16[64,768]{1,0:T(8,128)(2,1)}), bf16[1024,768]{1,0:T(8,128)(2,1)}) %all-gather.5.cloned.1.call-update) | async-done | bytes 1572880 | tf_op jit(solution)/shard_map/all_gather | solution.py:29
  99.0 5.6 exponential_convert_fusion
  104.6 1.7 fusion.5
  106.4 20.2 %psum.133 = f32[1024]{0:T(1024)S(1)} all-reduce(f32[1024]{0:T(1024)S(1)} %bitcast.122), channel_id=1, replica_groups=mesh['src'=16,'tgt'=8] {'tgt'}, use_global_device_ids=true, to_apply=%region_0.0 | all-reduce | flops 1024 | bytes 8192 | tf_op jit(solution)/shard_map/psum | solution.py:12
  126.6 0.9 fusion.10
  127.5 30.5 %psum.134 = f32[1024]{0:T(1024)S(1)} all-reduce(f32[1024]{0:T(1024)S(1)} %bitcast.123), channel_id=1, replica_groups=mesh['src'=16,'tgt'=8] {'src'}, use_global_device_ids=true, to_apply=%region_1.0 | all-reduce | flops 1024 | bytes 8192 | tf_op jit(solution)/shard_map/psum | solution.py:16
  158.0 1.7 fusion.11
  159.7 15.5 %psum.135 = f32[1024]{0:T(1024)S(1)} all-reduce(f32[1024]{0:T(1024)S(1)} %bitcast.124), channel_id=1, replica_groups=mesh['src'=16,'tgt'=8] {'tgt'}, use_global_device_ids=true, to_apply=%region_2.0 | all-reduce | flops 1024 | bytes 8192 | tf_op jit(solution)/shard_map/psum | solution.py:12
  175.2 0.9 fusion.12
  176.2 30.6 %psum.136 = f32[1024]{0:T(1024)S(1)} all-reduce(f32[1024]{0:T(1024)S(1)} %bitcast.125), channel_id=1, replica_groups=mesh['src'=16,'tgt'=8] {'src'}, use_global_device_ids=true, to_apply=%region_3.0 | all-reduce | flops 1024 | bytes 8192 | tf_op jit(solution)/shard_map/psum | solution.py:16
  206.8 1.7 fusion.13
  208.5 17.2 %psum.137 = f32[1024]{0:T(1024)S(1)} all-reduce(f32[1024]{0:T(1024)S(1)} %bitcast.126), channel_id=1, replica_groups=mesh['src'=16,'tgt'=8] {'tgt'}, use_global_device_ids=true, to_apply=%region_4.0 | all-reduce | flops 1024 | bytes 8192 | tf_op jit(solution)/shard_map/psum | solution.py:12
  225.7 0.9 fusion.14
  226.6 30.9 %psum.138 = f32[1024]{0:T(1024)S(1)} all-reduce(f32[1024]{0:T(1024)S(1)} %bitcast.127), channel_id=1, replica_groups=mesh['src'=16,'tgt'=8] {'src'}, use_global_device_ids=true, to_apply=%region_5.0 | all-reduce | flops 1024 | bytes 8192 | tf_op jit(solution)/shard_map/psum | solution.py:16
  257.5 1.7 fusion.15
  259.3 15.6 %psum.139 = f32[1024]{0:T(1024)S(1)} all-reduce(f32[1024]{0:T(1024)S(1)} %bitcast.128), channel_id=1, replica_groups=mesh['src'=16,'tgt'=8] {'tgt'}, use_global_device_ids=true, to_apply=%region_6.0 | all-reduce | flops 1024 | bytes 8192 | tf_op jit(solution)/shard_map/psum | solution.py:12
  274.9 0.9 fusion.16
  275.8 4.6 fusion.2
  280.5 31.1 %all-reduce = (f32[1024]{0:T(1024)S(1)}, f32[1024]{0:T(1024)S(1)}) all-reduce(f32[1024]{0:T(1024)S(1)} %bitcast.120, f32[1024]{0:T(1024)S(1)} %bitcast.121), channel_id=1, replica_groups=mesh['src'=16,'tgt'=8] {'src'}, use_global_device_ids=true, to_apply=%region_7.0 | all-reduce | flops 2048 | bytes 16384 | tf_op jit(solution)/shard_map/psum | solution.py:16
  311.6 6.1 fusion.1
  317.7 1.7 fusion.17
  319.4 17.2 %psum.152 = f32[1024]{0:T(1024)S(1)} all-reduce(f32[1024]{0:T(1024)S(1)} %add.58), channel_id=1, replica_groups=mesh['src'=16,'tgt'=8] {'tgt'}, use_global_device_ids=true, to_apply=%region_9.0 | all-reduce | flops 1024 | bytes 8192 | tf_op jit(solution)/shard_map/psum | solution.py:12
  336.7 0.9 fusion.18
  337.6 30.9 %psum.144 = f32[1024]{0:T(1024)S(1)} all-reduce(f32[1024]{0:T(1024)S(1)} %bitcast.129), channel_id=1, replica_groups=mesh['src'=16,'tgt'=8] {'src'}, use_global_device_ids=true, to_apply=%region_11.0 | all-reduce | flops 1024 | bytes 8192 | tf_op jit(solution)/shard_map/psum | solution.py:16
  368.5 1.7 fusion.19
  370.2 15.5 %psum.145 = f32[1024]{0:T(1024)S(1)} all-reduce(f32[1024]{0:T(1024)S(1)} %bitcast.130), channel_id=1, replica_groups=mesh['src'=16,'tgt'=8] {'tgt'}, use_global_device_ids=true, to_apply=%region_12.0 | all-reduce | flops 1024 | bytes 8192 | tf_op jit(solution)/shard_map/psum | solution.py:12
  385.7 0.9 fusion.20
  386.7 30.6 %psum.146 = f32[1024]{0:T(1024)S(1)} all-reduce(f32[1024]{0:T(1024)S(1)} %bitcast.131), channel_id=1, replica_groups=mesh['src'=16,'tgt'=8] {'src'}, use_global_device_ids=true, to_apply=%region_13.0 | all-reduce | flops 1024 | bytes 8192 | tf_op jit(solution)/shard_map/psum | solution.py:16
  417.3 1.7 fusion.21
  419.0 17.4 %psum.147 = f32[1024]{0:T(1024)S(1)} all-reduce(f32[1024]{0:T(1024)S(1)} %bitcast.132), channel_id=1, replica_groups=mesh['src'=16,'tgt'=8] {'tgt'}, use_global_device_ids=true, to_apply=%region_14.0 | all-reduce | flops 1024 | bytes 8192 | tf_op jit(solution)/shard_map/psum | solution.py:12
  436.4 0.9 fusion.22
  437.4 30.9 %psum.148 = f32[1024]{0:T(1024)S(1)} all-reduce(f32[1024]{0:T(1024)S(1)} %bitcast.133), channel_id=1, replica_groups=mesh['src'=16,'tgt'=8] {'src'}, use_global_device_ids=true, to_apply=%region_15.0 | all-reduce | flops 1024 | bytes 8192 | tf_op jit(solution)/shard_map/psum | solution.py:16
  468.3 1.7 fusion.23
  470.0 0.1 stack.64
  470.1 15.5 %psum.149 = f32[1024]{0:T(1024)S(1)} all-reduce(f32[1024]{0:T(1024)S(1)} %bitcast.119), channel_id=1, replica_groups=mesh['src'=16,'tgt'=8] {'tgt'}, use_global_device_ids=true, to_apply=%region_16.0 | all-reduce | flops 1024 | bytes 8192 | tf_op jit(solution)/shard_map/psum | solution.py:12
  485.6 0.1 stack.56
  485.7 6.2 fusion
  491.9 1.3 copy-done
  493.2 3.5 convolution_multiply_fusion.1
  496.8 1.5 copy-done.1
  498.3 5.0 convolution_multiply_fusion
  503.3 88.4 %all-reduce.4.cloned.1.call-done = f32[1024,768]{1,0:T(8,128)} async-done(((f32[1024,768]{1,0:T(8,128)}), f32[1024,768]{1,0:T(8,128)}) %all-reduce.4.cloned.1.call-update) | async-done | bytes 3145744 | tf_op jit(solution)/shard_map/psum | solution.py:90
  591.8 1.8 constant_dynamic-slice_fusion.1
  593.5 129.1 %all-reduce.6.cloned.1.call-done = f32[1024,768]{1,0:T(8,128)} async-done(((f32[1024,768]{1,0:T(8,128)}), f32[1024,768]{1,0:T(8,128)}) %all-reduce.6.cloned.1.call-update) | async-done | bytes 3145744 | tf_op jit(solution)/shard_map/psum | solution.py:91
  722.6 1.6 constant_dynamic-slice_fusion
  (31 shorter events, 0.3 us)
Async XLA Ops:
  7.2 56.0 %all-gather.3.cloned.1.call-start = ((), (), s32[]{:S(2)}) async-start(), calls=%async_computation | async-start | bytes 1769472 | tf_op jit(solution)/shard_map/all_gather | solution.py:28
  7.9 91.1 %all-gather.5.cloned.1.call-start = ((), (), s32[]{:S(2)}) async-start(), calls=%async_computation.1 | async-start | bytes 1671168 | tf_op jit(solution)/shard_map/all_gather | solution.py:29
  8.6 583.1 %all-reduce.4.cloned.1.call-start = ((), (), s32[]{:S(2)}) async-start(), calls=%async_computation.2 | async-start | bytes 6291456 | tf_op jit(solution)/shard_map/psum | solution.py:90
  104.6 21.9 %copy-start.2 = (f32[1024]{0:T(1024)S(1)}, f32[1024]{0:T(1024)}, u32[]{:S(2)}) copy-start(f32[1024]{0:T(1024)} %param.6) | copy-start | bytes 12292
  104.6 53.4 %copy-start.3 = (f32[1024]{0:T(1024)S(1)}, f32[1024]{0:T(1024)}, u32[]{:S(2)}) copy-start(f32[1024]{0:T(1024)} %param.7) | copy-start | bytes 12292
  485.6 7.6 %copy-start.4 = (bf16[1024,768]{1,0:T(8,128)(2,1)S(1)}, bf16[1024,768]{1,0:T(8,128)(2,1)}, u32[]{:S(2)}) copy-start(bf16[1024,768]{1,0:T(8,128)(2,1)} %all-gather.5.cloned.1.call-done) | copy-start | bytes 4718596
  491.9 1.3 copy-start
  496.7 1.6 copy-start.1
  496.8 225.9 %all-reduce.6.cloned.1.call-start = ((), (), s32[]{:S(2)}) async-start(), calls=%async_computation.3 | async-start | bytes 6291456 | tf_op jit(solution)/shard_map/psum | solution.py:91
Sparse Core Ops, SparseCore 0:
  10.3 52.8 all-gather.2
  64.9 34.0 all-gather.4
  496.9 94.8 all-reduce.3
  594.1 128.4 all-reduce.5
where the time goes:
time: 731 us
  blocking collectives  350 us (48%)
  waiting for transfers between devices  309 us (42%)
  matrix products  51.4 us (7%)
  between operations  13.9 us (2%)
    psum x7, blocking collectives, col_total(): return lax.psum(part, 'src')  216 us
    psum x8, blocking collectives, row_total(): return lax.psum(part, 'tgt')  134 us
    psum x1, waiting for transfers between devices, per_device(): tgt_whole = lax.psum(right_share_piece, 'src')  129 us
    psum x1, waiting for transfers between devices, per_device(): src_whole = lax.psum(left_share_piece, 'tgt')  88.4 us
    all_gather x1, waiting for transfers between devices, per_device(): src_rows = lax.all_gather(src_emb, 'tgt', axis=0, tiled=True)  54.5 us
    all_gather x1, waiting for transfers between devices, per_device(): lax.all_gather(right_sentence_vectors, 'src', axis=0, tiled=True)  35.8 us
    dot_general x9, matrix products, times_vector(): jnp.dot(kernel, vector, precision=highest, preferred_element_type=jnp.flo...  19.9 us
  transfers between devices with their start and end apart: 4, of which 4 were waited for; matrix products, arithmetic and copies ran while one was open for 1% of the time, Pallas kernels for 0%

commit v1 on v0

--- a/solution.py
+++ b/solution.py
@@ -26,7 +26,10 @@
 
 def per_device(src_emb, right_sentence_vectors, src_mass, tgt_mass):
     src_rows = lax.all_gather(src_emb, "tgt", axis=0, tiled=True)
-    target_rows = lax.all_gather(right_sentence_vectors, "src", axis=0, tiled=True)
+    target_rows = jnp.concatenate(
+        lax.all_to_all(jnp.stack([right_sentence_vectors] * lax.axis_size("src")), "src", 0, 0),
+        axis=0,
+    )
 
     def build():
         kernel_grid = (

time: 731 us -> 698 us (0.955)
  waiting for transfers between devices: 309 us -> 245 us
  blocking collectives: 350 us -> 380 us
    all_gather x1 -> x0, waiting for transfers between devices: 35.8 us -> none  [per_device(): lax.all_gather(right_sentence_vectors, 'src', axis=0, tiled=True)]
    all_to_all x0 -> x1, blocking collectives: none -> 30.9 us  [per_device(): lax.all_to_all(jnp.stack([right_sentence_vectors] * lax.axis_size('src'))...]
    all_gather x1, waiting for transfers between devices: 54.5 us -> 24.8 us  [per_device(): src_rows = lax.all_gather(src_emb, 'tgt', axis=0, tiled=True)]
  transfers between devices with their start and end apart: 4 -> 3, of which waited for: 4 -> 3; matrix products, arithmetic and copies ran while one was open for 1% -> 1% of each run, Pallas kernels for 0% -> 0%
where the time goes in v1:
time: 698 us
  blocking collectives  380 us (54%)
  waiting for transfers between devices  245 us (35%)
  matrix products  51.4 us (7%)
  between operations  13.9 us (2%)
  local copies, waits for them, and re-layouts  7.43 us (1%)
    psum x7, blocking collectives, col_total(): return lax.psum(part, 'src')  217 us
    psum x8, blocking collectives, row_total(): return lax.psum(part, 'tgt')  132 us
    psum x1, waiting for transfers between devices, per_device(): tgt_whole = lax.psum(right_share_piece, 'src')  129 us
    psum x1, waiting for transfers between devices, per_device(): src_whole = lax.psum(left_share_piece, 'tgt')  90.1 us
    all_to_all x1, blocking collectives, per_device(): lax.all_to_all(jnp.stack([right_sentence_vectors] * lax.axis_size('src'))...  30.9 us
    all_gather x1, waiting for transfers between devices, per_device(): src_rows = lax.all_gather(src_emb, 'tgt', axis=0, tiled=True)  24.8 us
    dot_general x9, matrix products, times_vector(): jnp.dot(kernel, vector, precision=highest, preferred_element_type=jnp.flo...  19.9 us
  transfers between devices with their start and end apart: 3, of which 3 were waited for; matrix products, arithmetic and copies ran while one was open for 1% of the time, Pallas kernels for 0%

profile of v1, /device:TPU:1, one launch (start us, length us, event | category | flops | bytes accessed | tf_op | source)
XLA Modules:
  0.0 697.6 jit_solution(11985994724924811937)
XLA Ops:
  7.2 0.7 all-gather.2.cloned.1.call-update
  7.9 1.0 stack.68
  9.0 30.9 %all_to_all.5 = bf16[16,64,768]{2,1,0:T(8,128)(2,1)} all-to-all(bf16[16,64,768]{2,1,0:T(8,128)(2,1)S(1)} %stack.68), channel_id=1, replica_groups=mesh['src'=16,'tgt'=8] {'src'}, dimensions={0} | all-to-all | bytes 3145728 | tf_op jit(solution)/shard_map/all_to_all | solution.py:30
  39.9 24.8 %all-gather.2.cloned.1.call-done = bf16[1024,768]{1,0:T(8,128)(2,1)} async-done(((bf16[128,768]{1,0:T(8,128)(2,1)}), bf16[1024,768]{1,0:T(8,128)(2,1)}) %all-gather.2.cloned.1.call-update) | async-done | bytes 1572880 | tf_op jit(solution)/shard_map/all_gather | solution.py:28
  64.6 5.7 exponential_convert_fusion
  70.3 1.7 fusion.5
  72.0 17.6 %psum.133 = f32[1024]{0:T(1024)S(1)} all-reduce(f32[1024]{0:T(1024)S(1)} %bitcast.125), channel_id=1, replica_groups=mesh['src'=16,'tgt'=8] {'tgt'}, use_global_device_ids=true, to_apply=%region_0.0 | all-reduce | flops 1024 | bytes 8192 | tf_op jit(solution)/shard_map/psum | solution.py:12
  89.6 0.9 fusion.10
  90.6 32.6 %psum.134 = f32[1024]{0:T(1024)S(1)} all-reduce(f32[1024]{0:T(1024)S(1)} %bitcast.126), channel_id=1, replica_groups=mesh['src'=16,'tgt'=8] {'src'}, use_global_device_ids=true, to_apply=%region_1.0 | all-reduce | flops 1024 | bytes 8192 | tf_op jit(solution)/shard_map/psum | solution.py:16
  123.1 1.7 fusion.11
  124.9 15.7 %psum.135 = f32[1024]{0:T(1024)S(1)} all-reduce(f32[1024]{0:T(1024)S(1)} %bitcast.127), channel_id=1, replica_groups=mesh['src'=16,'tgt'=8] {'tgt'}, use_global_device_ids=true, to_apply=%region_2.0 | all-reduce | flops 1024 | bytes 8192 | tf_op jit(solution)/shard_map/psum | solution.py:12
  140.6 0.9 fusion.12
  141.5 30.2 %psum.136 = f32[1024]{0:T(1024)S(1)} all-reduce(f32[1024]{0:T(1024)S(1)} %bitcast.128), channel_id=1, replica_groups=mesh['src'=16,'tgt'=8] {'src'}, use_global_device_ids=true, to_apply=%region_3.0 | all-reduce | flops 1024 | bytes 8192 | tf_op jit(solution)/shard_map/psum | solution.py:16
  171.8 1.7 fusion.13
  173.5 17.2 %psum.137 = f32[1024]{0:T(1024)S(1)} all-reduce(f32[1024]{0:T(1024)S(1)} %bitcast.129), channel_id=1, replica_groups=mesh['src'=16,'tgt'=8] {'tgt'}, use_global_device_ids=true, to_apply=%region_4.0 | all-reduce | flops 1024 | bytes 8192 | tf_op jit(solution)/shard_map/psum | solution.py:12
  190.7 0.9 fusion.14
  191.6 30.9 %psum.138 = f32[1024]{0:T(1024)S(1)} all-reduce(f32[1024]{0:T(1024)S(1)} %bitcast.130), channel_id=1, replica_groups=mesh['src'=16,'tgt'=8] {'src'}, use_global_device_ids=true, to_apply=%region_5.0 | all-reduce | flops 1024 | bytes 8192 | tf_op jit(solution)/shard_map/psum | solution.py:16
  222.5 1.7 fusion.15
  224.2 15.6 %psum.139 = f32[1024]{0:T(1024)S(1)} all-reduce(f32[1024]{0:T(1024)S(1)} %bitcast.131), channel_id=1, replica_groups=mesh['src'=16,'tgt'=8] {'tgt'}, use_global_device_ids=true, to_apply=%region_6.0 | all-reduce | flops 1024 | bytes 8192 | tf_op jit(solution)/shard_map/psum | solution.py:12
  239.9 0.9 fusion.16
  240.8 4.6 fusion.2
  245.4 31.1 %all-reduce = (f32[1024]{0:T(1024)S(1)}, f32[1024]{0:T(1024)S(1)}) all-reduce(f32[1024]{0:T(1024)S(1)} %bitcast.123, f32[1024]{0:T(1024)S(1)} %bitcast.124), channel_id=1, replica_groups=mesh['src'=16,'tgt'=8] {'src'}, use_global_device_ids=true, to_apply=%region_7.0 | all-reduce | flops 2048 | bytes 16384 | tf_op jit(solution)/shard_map/psum | solution.py:16
  276.5 6.1 fusion.1
  282.7 1.7 fusion.17
  284.4 17.2 %psum.152 = f32[1024]{0:T(1024)S(1)} all-reduce(f32[1024]{0:T(1024)S(1)} %add.58), channel_id=1, replica_groups=mesh['src'=16,'tgt'=8] {'tgt'}, use_global_device_ids=true, to_apply=%region_9.0 | all-reduce | flops 1024 | bytes 8192 | tf_op jit(solution)/shard_map/psum | solution.py:12
  301.7 0.9 fusion.18
  302.6 30.9 %psum.144 = f32[1024]{0:T(1024)S(1)} all-reduce(f32[1024]{0:T(1024)S(1)} %bitcast.132), channel_id=1, replica_groups=mesh['src'=16,'tgt'=8] {'src'}, use_global_device_ids=true, to_apply=%region_11.0 | all-reduce | flops 1024 | bytes 8192 | tf_op jit(solution)/shard_map/psum | solution.py:16
  333.5 1.7 fusion.19
  335.2 15.5 %psum.145 = f32[1024]{0:T(1024)S(1)} all-reduce(f32[1024]{0:T(1024)S(1)} %bitcast.133), channel_id=1, replica_groups=mesh['src'=16,'tgt'=8] {'tgt'}, use_global_device_ids=true, to_apply=%region_12.0 | all-reduce | flops 1024 | bytes 8192 | tf_op jit(solution)/shard_map/psum | solution.py:12
  350.7 0.9 fusion.20
  351.7 30.6 %psum.146 = f32[1024]{0:T(1024)S(1)} all-reduce(f32[1024]{0:T(1024)S(1)} %bitcast.134), channel_id=1, replica_groups=mesh['src'=16,'tgt'=8] {'src'}, use_global_device_ids=true, to_apply=%region_13.0 | all-reduce | flops 1024 | bytes 8192 | tf_op jit(solution)/shard_map/psum | solution.py:16
  382.3 1.7 fusion.21
  384.0 17.4 %psum.147 = f32[1024]{0:T(1024)S(1)} all-reduce(f32[1024]{0:T(1024)S(1)} %bitcast.135), channel_id=1, replica_groups=mesh['src'=16,'tgt'=8] {'tgt'}, use_global_device_ids=true, to_apply=%region_14.0 | all-reduce | flops 1024 | bytes 8192 | tf_op jit(solution)/shard_map/psum | solution.py:12
  401.4 0.9 fusion.22
  402.4 30.9 %psum.148 = f32[1024]{0:T(1024)S(1)} all-reduce(f32[1024]{0:T(1024)S(1)} %bitcast.136), channel_id=1, replica_groups=mesh['src'=16,'tgt'=8] {'src'}, use_global_device_ids=true, to_apply=%region_15.0 | all-reduce | flops 1024 | bytes 8192 | tf_op jit(solution)/shard_map/psum | solution.py:16
  433.3 1.7 fusion.23
  435.0 0.1 stack.84
  435.1 15.5 %psum.149 = f32[1024]{0:T(1024)S(1)} all-reduce(f32[1024]{0:T(1024)S(1)} %bitcast.122), channel_id=1, replica_groups=mesh['src'=16,'tgt'=8] {'tgt'}, use_global_device_ids=true, to_apply=%region_16.0 | all-reduce | flops 1024 | bytes 8192 | tf_op jit(solution)/shard_map/psum | solution.py:12
  450.6 0.1 stack.76
  450.6 6.2 fusion
  456.9 1.3 copy-done
  458.2 3.5 convolution_multiply_fusion.1
  461.8 1.5 copy-done.1
  463.3 5.0 convolution_multiply_fusion
  468.3 90.1 %all-reduce.4.cloned.1.call-done = f32[1024,768]{1,0:T(8,128)} async-done(((f32[1024,768]{1,0:T(8,128)}), f32[1024,768]{1,0:T(8,128)}) %all-reduce.4.cloned.1.call-update) | async-done | bytes 3145744 | tf_op jit(solution)/shard_map/psum | solution.py:93
  558.5 1.8 constant_dynamic-slice_fusion.1
  560.2 129.2 %all-reduce.6.cloned.1.call-done = f32[1024,768]{1,0:T(8,128)} async-done(((f32[1024,768]{1,0:T(8,128)}), f32[1024,768]{1,0:T(8,128)}) %all-reduce.6.cloned.1.call-update) | async-done | bytes 3145744 | tf_op jit(solution)/shard_map/psum | solution.py:94
  689.5 1.6 constant_dynamic-slice_fusion
  (30 shorter events, 0.3 us)
Async XLA Ops:
  7.2 57.5 %all-gather.2.cloned.1.call-start = ((), (), s32[]{:S(2)}) async-start(), calls=%async_computation.1 | async-start | bytes 1769472 | tf_op jit(solution)/shard_map/all_gather | solution.py:28
  7.9 550.6 %all-reduce.4.cloned.1.call-start = ((), (), s32[]{:S(2)}) async-start(), calls=%async_computation.2 | async-start | bytes 6291456 | tf_op jit(solution)/shard_map/psum | solution.py:93
  70.3 19.3 %copy-start.3 = (f32[1024]{0:T(1024)S(1)}, f32[1024]{0:T(1024)}, u32[]{:S(2)}) copy-start(f32[1024]{0:T(1024)} %param.6) | copy-start | bytes 12292
  70.3 52.8 %copy-start.4 = (f32[1024]{0:T(1024)S(1)}, f32[1024]{0:T(1024)}, u32[]{:S(2)}) copy-start(f32[1024]{0:T(1024)} %param.7) | copy-start | bytes 12292
  450.6 7.6 %copy-start.2 = (bf16[16,64,768]{2,1,0:T(8,128)(2,1)S(1)}, bf16[16,64,768]{2,1,0:T(8,128)(2,1)}, u32[]{:S(2)}) copy-start(bf16[16,64,768]{2,1,0:T(8,128)(2,1)} %all_to_all.5) | copy-start | bytes 4718596
  456.9 1.3 copy-start
  461.7 1.6 copy-start.1
  461.8 227.7 %all-reduce.6.cloned.1.call-start = ((), (), s32[]{:S(2)}) async-start(), calls=%async_computation.3 | async-start | bytes 6291456 | tf_op jit(solution)/shard_map/psum | solution.py:94
Sparse Core Ops, SparseCore 0:
  10.3 54.2 all-gather.1
  461.9 96.5 all-reduce.3
  561.0 128.4 all-reduce.5
